TPU v7x, 256 devices: a whole 4x4x8 slice. The times are simulated.
256 devices in a mesh: seq: 128 (over z, y, x_lo, core), dp: 2 (over x_hi).
Axes of the slice: x: 4 (x_hi: 2, x_lo: 2; x = x_hi * 2 + x_lo), y: 4, z: 8, core: 2. Of those that a mesh axis runs over, the one named last changes fastest.
Arguments:
- frames: bfloat16 [2, 16384, 1024], P('dp', 'seq'), may hold values from -36 to 36
- kernel: bfloat16 [31, 1024], replicated, may hold values from -1 to 1
- norm_gain: float32 [1024], replicated, may hold values from 0.5 to 1.5
- router: bfloat16 [1024, 32], replicated, may hold values from -0.1875 to 0.1875
- experts: int32 [2, 16384, 2], P('dp', 'seq'), may hold values from 0 to 31, all different within a row; in each aligned block of 128 rows (0 to 127, 128 to 255, ..., all dimensions but the last counted through in order) at most 16 rows name the same one
- w_in: bfloat16 [128, 1024, 512], P('seq'), may hold values from -0.1875 to 0.1875
- w_out: bfloat16 [128, 512, 1024], P('seq'), may hold values from -0.125 to 0.125
- cotangent: bfloat16 [2, 16384, 1024], P('dp', 'seq'), may hold values from -8 to 8
Outputs:
- mixed: bfloat16 [2, 16384, 1024], P('dp', 'seq')
- grad_frames: bfloat16 [2, 16384, 1024], P('dp', 'seq')
- grad_kernel: float32 [31, 1024], replicated
- grad_gain: float32 [1024], replicated
- grad_router: float32 [1024, 32], replicated
- grad_w_in: float32 [128, 1024, 512], P('seq')
- grad_w_out: float32 [128, 512, 1024], P('seq')
Inputs may be any that keep to these rules, and one draw needn't show every extreme that they name: Each frame names 2 different experts; in each aligned block of 128 frames no expert is named more than 16 times, a bound that some block reaches.
All inputs are finite; a program needn't handle non-finite values.
Results may differ from a plain program's by a relative error of at most 0.0075.
Values may be sent and summed in bfloat16 or wider, within the bound.
No kernel may reach another device: no remote copies, remote signals or barrier semaphores. Data moves between devices by JAX's collectives and lax.ppermute only.
A program may use at most 128 MiB of HBM per device.

v0:
```python
import jax
import jax.numpy as jnp
from jax import lax
from jax.sharding import Mesh
from jax.sharding import PartitionSpec as P

eps = 1e-06
SEQ = ("z", "y", "xl", "c")
GRP = ("z", "y")


def padded_2(shard, axis, size, width):
    length = shard.shape[0]
    up = [(i, (i + 1) % size) for i in range(size - 1)]
    down = [(j, i) for i, j in up]
    last = lax.slice_in_dim(shard, length - width, length, axis=0)
    initial = lax.slice_in_dim(shard, 0, width, axis=0)
    before = lax.ppermute(last, axis, up)
    after = lax.ppermute(initial, axis, down)
    return jnp.concatenate([before, shard, after], axis=0)


def conv_forward(padded, kernel, row_count):
    summed = jnp.zeros((row_count, padded.shape[1]), jnp.float32)
    for offset in range(kernel.shape[0]):
        summed = summed + kernel[offset].astype(jnp.float32) * padded[
            offset : offset + row_count
        ].astype(jnp.float32)
    return summed


def conv_transpose(padded, kernel, row_count):
    length = kernel.shape[0]
    summed = jnp.zeros((row_count, padded.shape[1]), jnp.float32)
    for offset in range(length):
        start = length - 1 - offset
        summed = summed + kernel[offset].astype(jnp.float32) * padded[start : start + row_count]
    return summed


def kernel_terms(padded, upstream, length, row_count):
    return jnp.stack(
        [
            jnp.sum(padded[offset : offset + row_count].astype(jnp.float32) * upstream, axis=0)
            for offset in range(length)
        ]
    )


def normalize(summed, norm_gain):
    square = jnp.mean(summed * summed, axis=-1, keepdims=True)
    return summed * lax.rsqrt(square + eps) * norm_gain


def slot_numbers(expert_ids, expert_count):
    onehot = (expert_ids[:, None] == jnp.arange(expert_count, dtype=jnp.int32)[None, :]).astype(
        jnp.int32
    )
    ranks = jnp.cumsum(onehot, axis=0) - onehot
    return jnp.sum(ranks * onehot, axis=1)


def gate_values(normed_b, router, first_ids, second_ids):
    logits = jnp.dot(normed_b, router, preferred_element_type=jnp.float32)
    columns = jnp.arange(router.shape[1], dtype=jnp.int32)[None, :]
    pick_diff = (first_ids[:, None] == columns).astype(jnp.float32) - (
        second_ids[:, None] == columns
    ).astype(jnp.float32)
    gate_one = jax.nn.sigmoid(jnp.sum(logits * pick_diff, axis=1))
    return (gate_one, 1.0 - gate_one, pick_diff)


def swish_parts(pre_act):
    squash = jax.nn.sigmoid(pre_act)
    return (pre_act * squash, squash * (1.0 + pre_act * (1.0 - squash)))


def gate_backward(upstream, out_one, out_two, gate_one, gate_two, pick_diff, normed_b, router):
    grad_gap = (
        (jnp.sum(upstream * out_one, axis=1) - jnp.sum(upstream * out_two, axis=1))
        * gate_one
        * gate_two
    )
    grad_logits = (grad_gap[:, None] * pick_diff).astype(jnp.bfloat16)
    router_term = jnp.dot(normed_b.T, grad_logits, preferred_element_type=jnp.float32)
    normed_term = jnp.dot(grad_logits, router.T, preferred_element_type=jnp.float32)
    return (router_term, normed_term)


def body(frames, kernel, norm_gain, router, experts, w_in, w_out, cotangent):
    inputs_dev = frames[0]
    row_count = inputs_dev.shape[0]
    width = inputs_dev.shape[1]
    length = kernel.shape[0]
    half_width = length // 2
    expert_count = router.shape[1]
    top_count = experts.shape[2]
    capacity = 2 * row_count * top_count // expert_count
    seq_size = lax.psum(1, SEQ)
    in_weights = w_in[0]
    out_weights = w_out[0]
    padded = padded_2(inputs_dev, SEQ, seq_size, half_width)
    summed = inputs_dev.astype(jnp.float32) + conv_forward(padded, kernel, row_count)
    normed_b = normalize(summed, norm_gain).astype(jnp.bfloat16)
    choice_ids = experts[0]
    gate_one, gate_two, pick_diff = gate_values(
        normed_b, router, choice_ids[:, 0], choice_ids[:, 1]
    )
    flat_ids = choice_ids.reshape(-1)
    slot_index = slot_numbers(flat_ids, expert_count)
    position = flat_ids * capacity + slot_index
    dispatch_table = (
        lax.broadcasted_iota(jnp.int32, (expert_count * capacity, flat_ids.shape[0]), 0)
        == position[None, :]
    ).astype(jnp.bfloat16)
    upstream = cotangent[0].astype(jnp.float32)
    repeated = jnp.repeat(normed_b, top_count, axis=0)
    grad_assigned = jnp.stack([gate_one[:, None] * upstream, gate_two[:, None] * upstream], axis=1)
    grad_values = grad_assigned.reshape(row_count * top_count, width).astype(jnp.bfloat16)
    both = jnp.concatenate([repeated, grad_values], axis=1)
    packed = jnp.dot(dispatch_table, both, preferred_element_type=jnp.float32).astype(jnp.bfloat16)
    packed = packed.reshape(expert_count, capacity, 2 * width)
    arrived = lax.all_to_all(packed, GRP, split_axis=0, concat_axis=0, tiled=True)
    arrived = lax.all_gather(arrived, "xl", axis=0, tiled=False)
    arrived = lax.all_gather(arrived, "c", axis=0, tiled=False)
    rows_shape = arrived.shape
    flat = arrived.reshape(-1, 2 * width)
    flat_rows = flat[:, :width]
    flat_grads = flat[:, width:]
    pre_act = jnp.dot(flat_rows, in_weights, preferred_element_type=jnp.float32)
    hidden_f, slope = swish_parts(pre_act)
    hidden = hidden_f.astype(jnp.bfloat16)
    partial_rows = jnp.dot(hidden, out_weights, preferred_element_type=jnp.float32).astype(
        jnp.bfloat16
    )
    grad_hidden = jnp.dot(flat_grads, out_weights.T, preferred_element_type=jnp.float32)
    grad_pre = (grad_hidden * slope).astype(jnp.bfloat16)
    out_term = jnp.dot(hidden.T, flat_grads, preferred_element_type=jnp.float32)
    in_term = jnp.dot(flat_rows.T, grad_pre, preferred_element_type=jnp.float32)
    grad_part = jnp.dot(grad_pre, in_weights.T, preferred_element_type=jnp.float32).astype(
        jnp.bfloat16
    )
    dp_pair = [(0, 1), (1, 0)]
    in_mine, out_mine = (in_term.astype(jnp.bfloat16), out_term.astype(jnp.bfloat16))
    in_other = lax.ppermute(in_mine, "dp", dp_pair)
    out_other = lax.ppermute(out_mine, "dp", dp_pair)
    dp_first = lax.axis_index("dp") == 0
    in_a = jnp.where(dp_first, in_mine, in_other).astype(jnp.float32)
    in_b = jnp.where(dp_first, in_other, in_mine).astype(jnp.float32)
    out_a = jnp.where(dp_first, out_mine, out_other).astype(jnp.float32)
    out_b = jnp.where(dp_first, out_other, out_mine).astype(jnp.float32)
    grad_in = in_a + in_b
    grad_out = out_a + out_b
    back = jnp.concatenate([partial_rows, grad_part], axis=1).reshape(rows_shape)
    back = lax.psum_scatter(back, "c", scatter_dimension=0, tiled=True)
    back = lax.psum_scatter(back, "xl", scatter_dimension=1, tiled=True)
    back = back.reshape(expert_count, capacity, 2 * width)
    totals = lax.all_to_all(back, GRP, split_axis=0, concat_axis=0, tiled=True)
    totals = totals.reshape(expert_count * capacity, 2 * width)
    picked = jnp.take(totals, position, axis=0).astype(jnp.float32)
    picked = picked.reshape(row_count, top_count, 2 * width)
    out_one = picked[:, 0, :width]
    out_two = picked[:, 1, :width]
    normed_grads = picked[:, 0, width:] + picked[:, 1, width:]
    mixed = (summed + gate_one[:, None] * out_one + gate_two[:, None] * out_two).astype(
        jnp.bfloat16
    )
    router_term, normed_term = gate_backward(
        upstream, out_one, out_two, gate_one, gate_two, pick_diff, normed_b, router
    )
    pullback = jax.vjp(normalize, summed, norm_gain)[1]
    summed_grad, gain_term = pullback(normed_grads + normed_term)
    upstream_total = upstream + summed_grad
    padded_grad = padded_2(upstream_total.astype(jnp.bfloat16), SEQ, seq_size, half_width).astype(
        upstream_total.dtype
    )
    grad_frames = (upstream_total + conv_transpose(padded_grad, kernel, row_count)).astype(
        jnp.bfloat16
    )
    kernel_term = kernel_terms(padded, upstream_total, length, row_count)
    small = jnp.concatenate([kernel_term, gain_term[None, :], router_term.T], axis=0)
    for axis in ("c", "xl", "y", "z", "dp"):
        small = lax.psum(small, axis)
    grad_kernel = small[:length]
    grad_gain = small[length]
    grad_router = small[length + 1 :].T
    return (
        mixed[None],
        grad_frames[None],
        grad_kernel,
        grad_gain,
        grad_router,
        grad_in[None],
        grad_out[None],
    )


def solution(mesh):
    split_mesh = Mesh(mesh.devices.reshape(8, 4, 2, 2, 2), SEQ + ("dp",))
    return jax.shard_map(
        body,
        mesh=split_mesh,
        in_specs=(
            P("dp", SEQ, None),
            P(),
            P(),
            P(),
            P("dp", SEQ, None),
            P(SEQ, None, None),
            P(SEQ, None, None),
            P("dp", SEQ, None),
        ),
        out_specs=(
            P("dp", SEQ, None),
            P("dp", SEQ, None),
            P(),
            P(),
            P(),
            P(SEQ, None, None),
            P(SEQ, None, None),
        ),
        check_vma=False,
    )
```

profile of v0, /device:TPU:1, one launch (start us, length us, event | category | flops | bytes accessed | tf_op | source)
XLA Modules:
  0.0 620.3 jit_solution(765407525963802871)
XLA Ops:
  8.1 4.5 collective-permute-start
  12.6 1.9 collective-permute-start.1
  19.7 9.2 %multiply_reduce_fusion.2 = (f32[128]{0:T(128)S(1)}, f32[128,1024]{1,0:T(8,128)S(1)}) fusion(bf16[15,1024]{1,0:T(8,128)(2,1)S(1)} %collective-permute-done.1, bf16[128,1024]{1,0:T(8,128)(2,1)} %bitcast.175, f32[1024]{0:T(1024)S(1)} %bitcast.202, f32[1024]{0:T(1024)S(1)} %bitcast.204, f32[1024]{0:T(1024)S(1)} %bitcast.208, f32[1024]{0:T(1024)S(1)} %bitcast.210, ...), kind=kLoop, calls=%fused_computation.269 | loop fusion | flops 24248192 | bytes 975360 | tf_op jit(solution)/shard_map/reduce_sum | solution.py:51
  33.9 58.0 %all_to_all.10 = bf16[32,16,2048]{2,1,0:T(8,128)(2,1)} all-to-all(bf16[32,16,2048]{2,1,0:T(8,128)(2,1)S(1)} %bitcast.174), channel_id=1, replica_groups=mesh['z'=8,'y'=4,'xl'=2,'c'=2,'dp'=2] {'z','y'}, dimensions={0} | all-to-all | bytes 4194304 | tf_op jit(solution)/shard_map/all_to_all | solution.py:123
  92.0 63.6 %all-gather.5.cloned.1.call-done = bf16[64,16,2048]{2,1,0:T(8,128)(2,1)} async-done(((bf16[32,16,2048]{2,1,0:T(8,128)(2,1)}), bf16[64,16,2048]{2,1,0:T(8,128)(2,1)}) %all-gather.5.cloned.1.call-update) | async-done | bytes 4194320 | tf_op jit(solution)/shard_map/all_gather | solution.py:124
  155.8 28.6 %all-gather.7.cloned.1.call-done = bf16[4,32,16,2048]{3,2,1,0:T(8,128)(2,1)} async-done(((bf16[2,32,16,2048]{3,2,1,0:T(8,128)(2,1)}), bf16[4,32,16,2048]{3,2,1,0:T(8,128)(2,1)}) %all-gather.7.cloned.1.call-update) | async-done | bytes 8388624 | tf_op jit(solution)/shard_map/all_gather | solution.py:125
  184.5 4.7 fusion.6
  189.2 3.6 multiply_convert_fusion
  192.8 4.5 convolution_convert_fusion.1
  197.3 4.3 convolution_convert_fusion
  201.6 8.3 %pad_maximum_fusion = bf16[2048,2048]{0,1:T(8,128)(2,1)} fusion(bf16[2048,1024]{0,1:T(8,128)(2,1)} %convolution_convert_fusion, bf16[2048,1024]{0,1:T(8,128)(2,1)} %convolution_convert_fusion.1), kind=kLoop, calls=%fused_computation.1 | loop fusion | flops 16777216 | bytes 16777216 | tf_op jit(solution)/shard_map/concatenate | solution.py:154
  210.0 12.3 %copy.48 = bf16[2048,2048]{1,0:T(8,128)(2,1)} copy(bf16[2048,2048]{0,1:T(8,128)(2,1)} %pad_maximum_fusion) | data formatting | bytes 16777216 | tf_op jit(solution)/shard_map/concatenate | solution.py:154
  222.3 23.1 %reduce-scatter.3.cloned.1.call-done = bf16[1,2,32,16,2048]{4,3,2,1,0:T(8,128)(2,1)} async-done(((bf16[2,2,32,16,2048]{4,3,2,1,0:T(8,128)(2,1)}), bf16[1,2,32,16,2048]{4,3,2,1,0:T(8,128)(2,1)}) %reduce-scatter.3.cloned.1.call-update) | async-done | bytes 4194320 | tf_op jit(solution)/shard_map/reduce_scatter | solution.py:155
  245.4 62.4 %reduce-scatter.5.cloned.1.call-done = bf16[1,1,32,16,2048]{4,3,2,1,0:T(8,128)(2,1)} async-done(((bf16[1,2,32,16,2048]{4,3,2,1,0:T(8,128)(2,1)}), bf16[1,1,32,16,2048]{4,3,2,1,0:T(8,128)(2,1)}) %reduce-scatter.5.cloned.1.call-update) | async-done | bytes 2097168 | tf_op jit(solution)/shard_map/reduce_scatter | solution.py:156
  307.8 9.6 %all-to-all-start.1 = ((bf16[32,16,2048]{2,1,0:T(8,128)(2,1)}), bf16[32,16,2048]{2,1,0:T(8,128)(2,1)S(1)}, u32[]{:S(2)}, u32[]{:S(2)}) async-start(bf16[32,16,2048]{2,1,0:T(8,128)(2,1)} %bitcast.181), calls=%async_computation.3 | async-start | bytes 4194304 | tf_op jit(solution)/shard_map/all_to_all | solution.py:158
  318.5 6.9 %fusion.11 = bf16[512,1024]{1,0:T(8,128)(2,1)} fusion(bf16[2048,2048]{1,0:T(8,128)(2,1)} %bitcast.281, f32[2048,512]{1,0:T(8,128)} %copy-done.48), kind=kOutput, calls=%fused_computation.47 | convolution fusion | flops 2153250816 | bytes 9437184 | tf_op jit(solution)/shard_map/dot_general | solution.py:138
  325.5 2.4 collective-permute-start.5
  327.8 38.0 %all-to-all-done.1 = bf16[32,16,2048]{2,1,0:T(8,128)(2,1)S(1)} async-done(((bf16[32,16,2048]{2,1,0:T(8,128)(2,1)}), bf16[32,16,2048]{2,1,0:T(8,128)(2,1)S(1)}, u32[]{:S(2)}, u32[]{:S(2)}) %all-to-all-start.1) | async-done | bytes 2097184 | tf_op jit(solution)/shard_map/all_to_all | solution.py:158
  365.8 2.3 gather_fusion
  375.7 3.3 concatenate.52
  379.1 5.2 fusion.8
  384.3 2.5 collective-permute-start.4
  386.8 21.3 %all-reduce.6.cloned.1.call-done = f32[64,1024]{1,0:T(8,128)} async-done(((f32[64,1024]{1,0:T(8,128)}), f32[64,1024]{1,0:T(8,128)}) %all-reduce.6.cloned.1.call-update) | async-done | bytes 262160 | tf_op jit(solution)/shard_map/psum | solution.py:183
  408.1 37.5 %all-reduce.8.cloned.1.call-done = f32[64,1024]{1,0:T(8,128)} async-done(((f32[64,1024]{1,0:T(8,128)}), f32[64,1024]{1,0:T(8,128)}) %all-reduce.8.cloned.1.call-update) | async-done | bytes 262160 | tf_op jit(solution)/shard_map/psum | solution.py:183
  445.8 3.3 add_bitcast_fusion
  449.1 3.5 collective-permute-start.2
  452.6 1.9 collective-permute-start.3
  454.6 39.8 %all-reduce.10.cloned.1.call-done = f32[64,1024]{1,0:T(8,128)} async-done(((f32[64,1024]{1,0:T(8,128)}), f32[64,1024]{1,0:T(8,128)}) %all-reduce.10.cloned.1.call-update) | async-done | bytes 262160 | tf_op jit(solution)/shard_map/psum | solution.py:183
  494.4 2.9 add_bitcast_fusion.1
  497.4 69.7 %all-reduce.12.cloned.1.call-done = f32[64,1024]{1,0:T(8,128)} async-done(((f32[64,1024]{1,0:T(8,128)}), f32[64,1024]{1,0:T(8,128)}) %all-reduce.12.cloned.1.call-update) | async-done | bytes 262160 | tf_op jit(solution)/shard_map/psum | solution.py:183
  567.3 2.8 fusion.158
  570.1 39.2 %all-reduce.14.cloned.1.call-done = f32[64,1024]{1,0:T(8,128)} async-done(((f32[64,1024]{1,0:T(8,128)}), f32[64,1024]{1,0:T(8,128)}) %all-reduce.14.cloned.1.call-update) | async-done | bytes 262160 | tf_op jit(solution)/shard_map/psum | solution.py:183
  (173 shorter events, 24.4 us)
Async XLA Ops:
  7.2 182.0 %copy-start = (bf16[1,512,1024]{2,1,0:T(8,128)(2,1)S(1)}, bf16[1,512,1024]{2,1,0:T(8,128)(2,1)}, u32[]{:S(2)}) copy-start(bf16[1,512,1024]{2,1,0:T(8,128)(2,1)} %param.14) | copy-start | bytes 3145732
  7.2 148.4 %all-gather.5.cloned.1.call-start = ((), (), s32[]{:S(2)}) async-start(), calls=%async_computation.11 | async-start | bytes 6291456 | tf_op jit(solution)/shard_map/all_gather | solution.py:124
  8.1 11.6 %collective-permute-start = (bf16[15,1024]{1,0:T(8,128)(2,1)S(1)}, bf16[15,1024]{1,0:T(8,128)(2,1)S(1)}, u32[]{:S(2)}, u32[]{:S(2)}) collective-permute-start(bf16[15,1024]{1,0:T(8,128)(2,1)S(1)} %get-tuple-element.53), channel_id=1, source_target_pairs={{0,2},{2,4},{4,6},{6,8},{8,10},{10,12},{12,14},{14,16},{16,18},{18... | collective-permute-start | bytes 92168 | tf_op jit(solution)/shard_map/ppermute | solution.py:18
  12.6 7.1 %collective-permute-start.1 = (bf16[15,1024]{1,0:T(8,128)(2,1)S(1)}, bf16[15,1024]{1,0:T(8,128)(2,1)S(1)}, u32[]{:S(2)}, u32[]{:S(2)}) collective-permute-start(bf16[15,1024]{1,0:T(8,128)(2,1)S(1)} %get-tuple-element.54), channel_id=1, source_target_pairs={{2,0},{4,2},{6,4},{8,6},{10,8},{12,10},{14,12},{16,14},{18,16},{20... | collective-permute-start | bytes 92168 | tf_op jit(solution)/shard_map/ppermute | solution.py:19
  91.9 92.6 %copy-start.47 = (bf16[1,1024,512]{2,1,0:T(8,128)(2,1)S(1)}, bf16[1,1024,512]{2,1,0:T(8,128)(2,1)}, u32[]{:S(2)}) copy-start(bf16[1,1024,512]{2,1,0:T(8,128)(2,1)} %param.13) | copy-start | bytes 3145732
  91.9 92.5 %all-gather.7.cloned.1.call-start = ((), (), s32[]{:S(2)}) async-start(), calls=%async_computation.12 | async-start | bytes 12582912 | tf_op jit(solution)/shard_map/all_gather | solution.py:125
  155.6 89.8 %reduce-scatter.3.cloned.1.call-start = ((), (), s32[]{:S(2)}) async-start(), calls=%async_computation.4 | async-start | bytes 12582912 | tf_op jit(solution)/shard_map/reduce_scatter | solution.py:155
  222.3 85.5 %reduce-scatter.5.cloned.1.call-start = ((), (), s32[]{:S(2)}) async-start(), calls=%async_computation.5 | async-start | bytes 6291456 | tf_op jit(solution)/shard_map/reduce_scatter | solution.py:156
  245.4 72.1 %copy-start.32 = (s32[256]{0:T(256)S(1)}, s32[256]{0:T(256)}, u32[]{:S(2)}) copy-start(s32[256]{0:T(256)} %copy-done.31) | copy-start | bytes 3076
  245.4 72.2 %copy-start.33 = (s32[1,128,2]{1,2,0:T(2,128)S(1)}, s32[1,128,2]{1,2,0:T(2,128)}, u32[]{:S(2)}) copy-start(s32[1,128,2]{1,2,0:T(2,128)} %param.12) | copy-start | bytes 3076
  307.8 58.0 %all-to-all-start.1 = ((bf16[32,16,2048]{2,1,0:T(8,128)(2,1)}), bf16[32,16,2048]{2,1,0:T(8,128)(2,1)S(1)}, u32[]{:S(2)}, u32[]{:S(2)}) async-start(bf16[32,16,2048]{2,1,0:T(8,128)(2,1)} %bitcast.181), calls=%async_computation.3 | async-start | bytes 4194304 | tf_op jit(solution)/shard_map/all_to_all | solution.py:158
  317.4 90.6 %all-reduce.6.cloned.1.call-start = ((), (), s32[]{:S(2)}) async-start(), calls=%async_computation.6 | async-start | bytes 524288 | tf_op jit(solution)/shard_map/psum | solution.py:183
  325.5 120.4 %collective-permute-start.5 = (bf16[512,1024]{1,0:T(8,128)(2,1)}, bf16[512,1024]{1,0:T(8,128)(2,1)}, u32[]{:S(2)}, u32[]{:S(2)}) collective-permute-start(bf16[512,1024]{1,0:T(8,128)(2,1)} %fusion.11), channel_id=1, source_target_pairs={{0,1},{1,0},{2,3},{3,2},{4,5},{5,4},{6,7},{7,6},{8,9},{9,8},{10,11... | collective-permute-start | bytes 3145736 | tf_op jit(solution)/shard_map/ppermute | solution.py:146
  379.0 66.6 %all-reduce.8.cloned.1.call-start = ((), (), s32[]{:S(2)}) async-start(), calls=%async_computation.7 | async-start | bytes 524288 | tf_op jit(solution)/shard_map/psum | solution.py:183
  384.3 110.1 %collective-permute-start.4 = (bf16[1024,512]{1,0:T(8,128)(2,1)S(1)}, bf16[1024,512]{1,0:T(8,128)(2,1)}, u32[]{:S(2)}, u32[]{:S(2)}) collective-permute-start(bf16[1024,512]{1,0:T(8,128)(2,1)S(1)} %fusion.8), channel_id=1, source_target_pairs={{0,1},{1,0},{2,3},{3,2},{4,5},{5,4},{6,7},{7,6},{8,9},{9,8},{10,11... | collective-permute-start | bytes 3145736 | tf_op jit(solution)/shard_map/ppermute | solution.py:145
  408.1 86.3 %all-reduce.10.cloned.1.call-start = ((), (), s32[]{:S(2)}) async-start(), calls=%async_computation.8 | async-start | bytes 524288 | tf_op jit(solution)/shard_map/psum | solution.py:183
  445.7 121.6 %copy-start.10 = (f32[1,1024]{1,0:T(1,128)S(1)}, f32[1,1024]{1,0:T(1,128)}, u32[]{:S(2)}) copy-start(f32[1,1024]{1,0:T(1,128)} %copy-done.9) | copy-start | bytes 12292
  445.7 121.6 %copy-start.12 = (f32[1,1024]{1,0:T(1,128)S(1)}, f32[1,1024]{1,0:T(1,128)}, u32[]{:S(2)}) copy-start(f32[1,1024]{1,0:T(1,128)} %copy-done.11) | copy-start | bytes 12292
  445.7 121.5 %copy-start.14 = (f32[1,1024]{1,0:T(1,128)S(1)}, f32[1,1024]{1,0:T(1,128)}, u32[]{:S(2)}) copy-start(f32[1,1024]{1,0:T(1,128)} %copy-done.13) | copy-start | bytes 12292
  445.7 121.5 %copy-start.16 = (f32[1,1024]{1,0:T(1,128)S(1)}, f32[1,1024]{1,0:T(1,128)}, u32[]{:S(2)}) copy-start(f32[1,1024]{1,0:T(1,128)} %copy-done.15) | copy-start | bytes 12292
  445.7 121.5 %copy-start.18 = (f32[1,1024]{1,0:T(1,128)S(1)}, f32[1,1024]{1,0:T(1,128)}, u32[]{:S(2)}) copy-start(f32[1,1024]{1,0:T(1,128)} %copy-done.17) | copy-start | bytes 12292
  445.7 121.5 %copy-start.20 = (f32[1,1024]{1,0:T(1,128)S(1)}, f32[1,1024]{1,0:T(1,128)}, u32[]{:S(2)}) copy-start(f32[1,1024]{1,0:T(1,128)} %copy-done.19) | copy-start | bytes 12292
  445.7 121.5 %copy-start.22 = (f32[1,1024]{1,0:T(1,128)S(1)}, f32[1,1024]{1,0:T(1,128)}, u32[]{:S(2)}) copy-start(f32[1,1024]{1,0:T(1,128)} %copy-done.21) | copy-start | bytes 12292
  445.7 121.5 %copy-start.24 = (f32[1,1024]{1,0:T(1,128)S(1)}, f32[1,1024]{1,0:T(1,128)}, u32[]{:S(2)}) copy-start(f32[1,1024]{1,0:T(1,128)} %copy-done.23) | copy-start | bytes 12292
  445.7 121.5 %copy-start.26 = (f32[1,1024]{1,0:T(1,128)S(1)}, f32[1,1024]{1,0:T(1,128)}, u32[]{:S(2)}) copy-start(f32[1,1024]{1,0:T(1,128)} %copy-done.25) | copy-start | bytes 12292
  445.7 121.5 %copy-start.28 = (f32[1,1024]{1,0:T(1,128)S(1)}, f32[1,1024]{1,0:T(1,128)}, u32[]{:S(2)}) copy-start(f32[1,1024]{1,0:T(1,128)} %copy-done.27) | copy-start | bytes 12292
  445.8 121.5 %copy-start.30 = (f32[1,1024]{1,0:T(1,128)S(1)}, f32[1,1024]{1,0:T(1,128)}, u32[]{:S(2)}) copy-start(f32[1,1024]{1,0:T(1,128)} %copy-done.29) | copy-start | bytes 12292
  445.8 121.4 %all-reduce.12.cloned.1.call-start = ((), (), s32[]{:S(2)}) async-start(), calls=%async_computation.9 | async-start | bytes 524288 | tf_op jit(solution)/shard_map/psum | solution.py:183
  449.1 48.2 %collective-permute-start.2 = (bf16[15,1024]{1,0:T(8,128)(2,1)S(1)}, bf16[15,1024]{1,0:T(8,128)(2,1)S(1)}, u32[]{:S(2)}, u32[]{:S(2)}) collective-permute-start(bf16[15,1024]{1,0:T(8,128)(2,1)S(1)} %get-tuple-element.49), channel_id=1, source_target_pairs={{0,2},{2,4},{4,6},{6,8},{8,10},{10,12},{12,14},{14,16},{16,18},{18... | collective-permute-start | bytes 92168 | tf_op jit(solution)/shard_map/ppermute | solution.py:18
  452.6 44.7 %collective-permute-start.3 = (bf16[15,1024]{1,0:T(8,128)(2,1)S(1)}, bf16[15,1024]{1,0:T(8,128)(2,1)S(1)}, u32[]{:S(2)}, u32[]{:S(2)}) collective-permute-start(bf16[15,1024]{1,0:T(8,128)(2,1)S(1)} %get-tuple-element.50), channel_id=1, source_target_pairs={{2,0},{4,2},{6,4},{8,6},{10,8},{12,10},{14,12},{16,14},{18,16},{20... | collective-permute-start | bytes 92168 | tf_op jit(solution)/shard_map/ppermute | solution.py:19
  494.4 114.9 %all-reduce.14.cloned.1.call-start = ((), (), s32[]{:S(2)}) async-start(), calls=%async_computation.10 | async-start | bytes 524288 | tf_op jit(solution)/shard_map/psum | solution.py:183
  567.3 46.5 %copy-start.1 = (bf16[1,512,1024]{2,1,0:T(8,128)(2,1)S(1)}, bf16[1,512,1024]{2,1,0:T(8,128)(2,1)}, u32[]{:S(2)}) copy-start(bf16[1,512,1024]{2,1,0:T(8,128)(2,1)} %param.14) | copy-start | bytes 3145732
  (34 other events, 249.9 us)
Sparse Core Ops, SparseCore 0:
  92.1 63.4 all-gather.4
  157.4 27.0 all-gather.6
  222.4 22.9 reduce-scatter.2
  247.8 59.9 reduce-scatter.4
  379.2 28.8 all-reduce.5
  410.5 35.0 all-reduce.7
  447.9 46.3 all-reduce.9
  496.7 70.4 all-reduce.11
  569.8 39.5 all-reduce.13
where the time goes:
time: 621 us; the launch traced here: 620 us
  waiting for transfers between devices  423 us (68%)
  blocking collectives  58 us (9%)
  other arithmetic  36 us (6%)
  matrix products  31.6 us (5%)
  local copies, waits for them, and re-layouts  29.8 us (5%)
  starting transfers between devices  26.8 us (4%)
  between operations  14.8 us (2%)
    psum x5, waiting for transfers between devices, body(): small = lax.psum(small, axis)  208 us
    all_gather x1, waiting for transfers between devices, body(): arrived = lax.all_gather(arrived, 'xl', axis=0, tiled=False)  63.6 us
    reduce_scatter x1, waiting for transfers between devices, body(): back = lax.psum_scatter(back, 'xl', scatter_dimension=1, tiled=True)  62.4 us
    all_to_all x1, blocking collectives, body(): lax.all_to_all(packed, GRP, split_axis=0, concat_axis=0, tiled=True)  58 us
    all_to_all x1, waiting for transfers between devices, body(): totals = lax.all_to_all(back, GRP, split_axis=0, concat_axis=0, tiled=True)  38 us
    all_gather x1, waiting for transfers between devices, body(): arrived = lax.all_gather(arrived, 'c', axis=0, tiled=False)  28.6 us
    reduce_scatter x1, waiting for transfers between devices, body(): back = lax.psum_scatter(back, 'c', scatter_dimension=0, tiled=True)  23.1 us
  transfers between devices with their start and end apart: 16, of which 10 were waited for; matrix products, arithmetic and copies ran while one was open for 6% of the time, Pallas kernels for 0%

commit v1 on v0

--- a/solution.py
+++ b/solution.py
@@ -180,7 +180,7 @@
     kernel_term = kernel_terms(padded, upstream_total, length, row_count)
     small = jnp.concatenate([kernel_term, gain_term[None, :], router_term.T], axis=0)
     for axis in ("c", "xl", "y", "z", "dp"):
-        small = lax.psum(small, axis)
+        small = jnp.sum(lax.all_gather(small, axis), axis=0)
     grad_kernel = small[:length]
     grad_gain = small[length]
     grad_router = small[length + 1 :].T

time: 621 us -> 498 us (0.80)
  waiting for transfers between devices: 423 us -> 272 us
  blocking collectives: 58 us -> 78.1 us
  other arithmetic: 36 us -> 42.6 us
    psum x5 -> x0, waiting for transfers between devices: 208 us -> none  [body(): small = lax.psum(small, axis)]
    all_gather x0 -> x2, waiting for transfers between devices: none -> 22.3 us  [body(): small = jnp.sum(lax.all_gather(small, axis), axis=0)]
    all_gather x0 -> x3, blocking collectives: none -> 20.1 us  [body(): small = jnp.sum(lax.all_gather(small, axis), axis=0)]
    ppermute x1, waiting for transfers between devices: 0.01 us -> 16.1 us  [body(): out_other = lax.ppermute(out_mine, 'dp', dp_pair)]
    all_to_all x1, waiting for transfers between devices: 38 us -> 47.1 us  [body(): totals = lax.all_to_all(back, GRP, split_axis=0, concat_axis=0, tiled=True)]
    ppermute x1, waiting for transfers between devices: 0.01 us -> 7.45 us  [body(): in_other = lax.ppermute(in_mine, 'dp', dp_pair)]
    ppermute x2, starting transfers between devices: 8.02 us -> 14.3 us  [padded_2(): before = lax.ppermute(last, axis, up)]
  transfers between devices with their start and end apart: 16 -> 13, of which waited for: 10 -> 9; matrix products, arithmetic and copies ran while one was open for 6% -> 5% of each run, Pallas kernels for 0% -> 0%
where the time goes in v1:
time: 498 us; the launch traced here: 494 us
  waiting for transfers between devices  272 us (55%)
  blocking collectives  78.1 us (16%)
  other arithmetic  42.6 us (9%)
  starting transfers between devices  31.4 us (6%)
  matrix products  30.9 us (6%)
  local copies, waits for them, and re-layouts  24.1 us (5%)
  between operations  15.1 us (3%)
    all_gather x1, waiting for transfers between devices, body(): arrived = lax.all_gather(arrived, 'xl', axis=0, tiled=False)  63.6 us
    reduce_scatter x1, waiting for transfers between devices, body(): back = lax.psum_scatter(back, 'xl', scatter_dimension=1, tiled=True)  62.4 us
    all_to_all x1, blocking collectives, body(): lax.all_to_all(packed, GRP, split_axis=0, concat_axis=0, tiled=True)  58 us
    all_to_all x1, waiting for transfers between devices, body(): totals = lax.all_to_all(back, GRP, split_axis=0, concat_axis=0, tiled=True)  47.1 us
    all_gather x1, waiting for transfers between devices, body(): arrived = lax.all_gather(arrived, 'c', axis=0, tiled=False)  28.6 us
    reduce_scatter x1, waiting for transfers between devices, body(): back = lax.psum_scatter(back, 'c', scatter_dimension=0, tiled=True)  23.1 us
    all_gather x2, waiting for transfers between devices, body(): small = jnp.sum(lax.all_gather(small, axis), axis=0)  22.3 us
    all_gather x3, blocking collectives, body(): small = jnp.sum(lax.all_gather(small, axis), axis=0)  20.1 us
  transfers between devices with their start and end apart: 13, of which 9 were waited for; matrix products, arithmetic and copies ran while one was open for 5% of the time, Pallas kernels for 0%

profile of v1, /device:TPU:1, one launch (start us, length us, event | category | flops | bytes accessed | tf_op | source)
XLA Modules:
  0.0 494.0 jit_solution(8661614581285304783)
XLA Ops:
  8.1 4.5 collective-permute-start
  12.6 1.9 collective-permute-start.1
  19.7 11.3 %multiply_reduce_fusion.2 = (f32[128]{0:T(128)S(1)}, f32[128,1024]{1,0:T(8,128)S(1)}) fusion(bf16[15,1024]{1,0:T(8,128)(2,1)S(1)} %collective-permute-done.1, bf16[128,1024]{1,0:T(8,128)(2,1)} %bitcast.180, f32[1024]{0:T(1024)S(1)} %bitcast.212, f32[1024]{0:T(1024)S(1)} %bitcast.214, f32[1024]{0:T(1024)S(1)} %bitcast.218, f32[1024]{0:T(1024)S(1)} %bitcast.220, ...), kind=kLoop, calls=%fused_computation.269 | loop fusion | flops 24248192 | bytes 975360 | tf_op jit(solution)/shard_map/reduce_sum | solution.py:51
  36.0 58.0 %all_to_all.10 = bf16[32,16,2048]{2,1,0:T(8,128)(2,1)} all-to-all(bf16[32,16,2048]{2,1,0:T(8,128)(2,1)S(1)} %bitcast.179), channel_id=1, replica_groups=mesh['z'=8,'y'=4,'xl'=2,'c'=2,'dp'=2] {'z','y'}, dimensions={0} | all-to-all | bytes 4194304 | tf_op jit(solution)/shard_map/all_to_all | solution.py:123
  94.0 63.6 %all-gather.12.cloned.1.call-done = bf16[64,16,2048]{2,1,0:T(8,128)(2,1)} async-done(((bf16[32,16,2048]{2,1,0:T(8,128)(2,1)}), bf16[64,16,2048]{2,1,0:T(8,128)(2,1)}) %all-gather.12.cloned.1.call-update) | async-done | bytes 4194320 | tf_op jit(solution)/shard_map/all_gather | solution.py:124
  157.9 28.6 %all-gather.14.cloned.1.call-done = bf16[4,32,16,2048]{3,2,1,0:T(8,128)(2,1)} async-done(((bf16[2,32,16,2048]{3,2,1,0:T(8,128)(2,1)}), bf16[4,32,16,2048]{3,2,1,0:T(8,128)(2,1)}) %all-gather.14.cloned.1.call-update) | async-done | bytes 8388624 | tf_op jit(solution)/shard_map/all_gather | solution.py:125
  186.5 4.7 fusion.6
  191.3 3.5 multiply_convert_fusion
  194.8 4.5 convolution_convert_fusion.1
  199.3 4.3 convolution_convert_fusion
  203.7 8.3 %pad_maximum_fusion = bf16[2048,2048]{0,1:T(8,128)(2,1)} fusion(bf16[2048,1024]{0,1:T(8,128)(2,1)} %convolution_convert_fusion, bf16[2048,1024]{0,1:T(8,128)(2,1)} %convolution_convert_fusion.1), kind=kLoop, calls=%fused_computation.1 | loop fusion | flops 16777216 | bytes 16777216 | tf_op jit(solution)/shard_map/concatenate | solution.py:154
  212.0 12.3 %copy.57 = bf16[2048,2048]{1,0:T(8,128)(2,1)} copy(bf16[2048,2048]{0,1:T(8,128)(2,1)} %pad_maximum_fusion) | data formatting | bytes 16777216 | tf_op jit(solution)/shard_map/concatenate | solution.py:154
  224.4 23.1 %reduce-scatter.3.cloned.1.call-done = bf16[1,2,32,16,2048]{4,3,2,1,0:T(8,128)(2,1)} async-done(((bf16[2,2,32,16,2048]{4,3,2,1,0:T(8,128)(2,1)}), bf16[1,2,32,16,2048]{4,3,2,1,0:T(8,128)(2,1)}) %reduce-scatter.3.cloned.1.call-update) | async-done | bytes 4194320 | tf_op jit(solution)/shard_map/reduce_scatter | solution.py:155
  247.5 62.4 %reduce-scatter.5.cloned.1.call-done = bf16[1,1,32,16,2048]{4,3,2,1,0:T(8,128)(2,1)} async-done(((bf16[1,2,32,16,2048]{4,3,2,1,0:T(8,128)(2,1)}), bf16[1,1,32,16,2048]{4,3,2,1,0:T(8,128)(2,1)}) %reduce-scatter.5.cloned.1.call-update) | async-done | bytes 2097168 | tf_op jit(solution)/shard_map/reduce_scatter | solution.py:156
  309.9 9.6 %all-to-all-start.1 = ((bf16[32,16,2048]{2,1,0:T(8,128)(2,1)}), bf16[32,16,2048]{2,1,0:T(8,128)(2,1)S(1)}, u32[]{:S(2)}, u32[]{:S(2)}) async-start(bf16[32,16,2048]{2,1,0:T(8,128)(2,1)} %bitcast.187), calls=%async_computation.3 | async-start | bytes 4194304 | tf_op jit(solution)/shard_map/all_to_all | solution.py:158
  320.8 47.1 %all-to-all-done.1 = bf16[32,16,2048]{2,1,0:T(8,128)(2,1)S(1)} async-done(((bf16[32,16,2048]{2,1,0:T(8,128)(2,1)}), bf16[32,16,2048]{2,1,0:T(8,128)(2,1)S(1)}, u32[]{:S(2)}, u32[]{:S(2)}) %all-to-all-start.1) | async-done | bytes 2097184 | tf_op jit(solution)/shard_map/all_to_all | solution.py:158
  367.9 2.3 gather_fusion
  378.0 4.5 all-gather.2
  382.6 8.2 %all-gather.3 = f32[128,1024]{1,0:T(8,128)S(1)} all-gather(f32[64,1024]{1,0:T(8,128)S(1)} %reduce_sum.443), channel_id=5, replica_groups=mesh['z'=8,'y'=4,'xl'=2,'c'=2,'dp'=2] {'xl'}, dimensions={0}, use_global_device_ids=true | all-gather | bytes 786432 | tf_op jit(solution)/shard_map/all_gather | solution.py:183
  391.5 22.3 %all-gather.16.cloned.1.call-done = f32[256,1024]{1,0:T(8,128)} async-done(((f32[64,1024]{1,0:T(8,128)}), f32[256,1024]{1,0:T(8,128)}) %all-gather.16.cloned.1.call-update) | async-done | bytes 1048592 | tf_op jit(solution)/shard_map/all_gather | solution.py:183
  413.9 2.0 reduce_sum.445
  415.9 7.0 %fusion.11 = bf16[512,1024]{1,0:T(8,128)(2,1)} fusion(bf16[2048,2048]{1,0:T(8,128)(2,1)} %bitcast.291, f32[2048,512]{1,0:T(8,128)} %copy-done.48), kind=kOutput, calls=%fused_computation.47 | convolution fusion | flops 2153250816 | bytes 9437184 | tf_op jit(solution)/shard_map/dot_general | solution.py:138
  422.9 2.7 collective-permute-start.5
  425.6 4.5 fusion.8
  430.6 16.1 %collective-permute-done.5 = bf16[512,1024]{1,0:T(8,128)(2,1)} collective-permute-done((bf16[512,1024]{1,0:T(8,128)(2,1)}, bf16[512,1024]{1,0:T(8,128)(2,1)}, u32[]{:S(2)}, u32[]{:S(2)}) %collective-permute-start.5) | collective-permute-done | bytes 1048608 | tf_op jit(solution)/shard_map/ppermute | solution.py:146
  446.7 3.3 add_bitcast_fusion
  450.0 9.8 %collective-permute-start.2 = (bf16[15,1024]{1,0:T(8,128)(2,1)S(1)}, bf16[15,1024]{1,0:T(8,128)(2,1)S(1)}, u32[]{:S(2)}, u32[]{:S(2)}) collective-permute-start(bf16[15,1024]{1,0:T(8,128)(2,1)S(1)} %get-tuple-element.49), channel_id=1, source_target_pairs={{0,2},{2,4},{4,6},{6,8},{8,10},{10,12},{12,14},{14,16},{16,18},{18... | collective-permute-start | bytes 92168 | tf_op jit(solution)/shard_map/ppermute | solution.py:18
  459.8 1.9 collective-permute-start.3
  461.7 7.4 %collective-permute-done.4 = bf16[1024,512]{1,0:T(8,128)(2,1)} collective-permute-done((bf16[1024,512]{1,0:T(8,128)(2,1)S(1)}, bf16[1024,512]{1,0:T(8,128)(2,1)}, u32[]{:S(2)}, u32[]{:S(2)}) %collective-permute-start.4) | collective-permute-done | bytes 1048608 | tf_op jit(solution)/shard_map/ppermute | solution.py:145
  469.1 2.9 add_bitcast_fusion.1
  473.3 2.8 fusion.158
  477.8 7.4 %all-gather.6 = f32[128,1024]{1,0:T(8,128)S(1)} all-gather(f32[64,1024]{1,0:T(8,128)S(1)} %reduce_sum.446), channel_id=8, replica_groups=mesh['z'=8,'y'=4,'xl'=2,'c'=2,'dp'=2] {'dp'}, dimensions={0}, use_global_device_ids=true | all-gather | bytes 786432 | tf_op jit(solution)/shard_map/all_gather | solution.py:183
  (174 shorter events, 26.0 us)
Async XLA Ops:
  7.2 184.1 %copy-start = (bf16[1,512,1024]{2,1,0:T(8,128)(2,1)S(1)}, bf16[1,512,1024]{2,1,0:T(8,128)(2,1)}, u32[]{:S(2)}) copy-start(bf16[1,512,1024]{2,1,0:T(8,128)(2,1)} %param.14) | copy-start | bytes 3145732
  7.2 27.0 %copy-start.5 = (bf16[1,128,1024]{2,1,0:T(8,128)(2,1)S(1)}, bf16[1,128,1024]{2,1,0:T(8,128)(2,1)}, u32[]{:S(2)}) copy-start(bf16[1,128,1024]{2,1,0:T(8,128)(2,1)} %param.15) | copy-start | bytes 786436
  7.2 150.4 %all-gather.12.cloned.1.call-start = ((), (), s32[]{:S(2)}) async-start(), calls=%async_computation.6 | async-start | bytes 6291456 | tf_op jit(solution)/shard_map/all_gather | solution.py:124
  8.1 11.6 %collective-permute-start = (bf16[15,1024]{1,0:T(8,128)(2,1)S(1)}, bf16[15,1024]{1,0:T(8,128)(2,1)S(1)}, u32[]{:S(2)}, u32[]{:S(2)}) collective-permute-start(bf16[15,1024]{1,0:T(8,128)(2,1)S(1)} %get-tuple-element.53), channel_id=1, source_target_pairs={{0,2},{2,4},{4,6},{6,8},{8,10},{10,12},{12,14},{14,16},{16,18},{18... | collective-permute-start | bytes 92168 | tf_op jit(solution)/shard_map/ppermute | solution.py:18
  12.6 7.1 %collective-permute-start.1 = (bf16[15,1024]{1,0:T(8,128)(2,1)S(1)}, bf16[15,1024]{1,0:T(8,128)(2,1)S(1)}, u32[]{:S(2)}, u32[]{:S(2)}) collective-permute-start(bf16[15,1024]{1,0:T(8,128)(2,1)S(1)} %get-tuple-element.54), channel_id=1, source_target_pairs={{2,0},{4,2},{6,4},{8,6},{10,8},{12,10},{14,12},{16,14},{18,16},{20... | collective-permute-start | bytes 92168 | tf_op jit(solution)/shard_map/ppermute | solution.py:19
  19.7 16.2 %copy-start.34 = (s32[128]{0:T(128)}, s32[128]{0:T(128)S(1)}, u32[]{:S(2)}) copy-start(s32[128]{0:T(128)S(1)} %get-tuple-element.86) | copy-start | bytes 1540
  19.7 16.2 %copy-start.36 = (s32[128]{0:T(128)}, s32[128]{0:T(128)S(1)}, u32[]{:S(2)}) copy-start(s32[128]{0:T(128)S(1)} %get-tuple-element.87) | copy-start | bytes 1540
  94.0 92.6 %copy-start.47 = (bf16[1,1024,512]{2,1,0:T(8,128)(2,1)S(1)}, bf16[1,1024,512]{2,1,0:T(8,128)(2,1)}, u32[]{:S(2)}) copy-start(bf16[1,1024,512]{2,1,0:T(8,128)(2,1)} %param.13) | copy-start | bytes 3145732
  94.0 92.5 %all-gather.14.cloned.1.call-start = ((), (), s32[]{:S(2)}) async-start(), calls=%async_computation.7 | async-start | bytes 12582912 | tf_op jit(solution)/shard_map/all_gather | solution.py:125
  157.7 89.8 %reduce-scatter.3.cloned.1.call-start = ((), (), s32[]{:S(2)}) async-start(), calls=%async_computation.4 | async-start | bytes 12582912 | tf_op jit(solution)/shard_map/reduce_scatter | solution.py:155
  224.3 85.6 %reduce-scatter.5.cloned.1.call-start = ((), (), s32[]{:S(2)}) async-start(), calls=%async_computation.5 | async-start | bytes 6291456 | tf_op jit(solution)/shard_map/reduce_scatter | solution.py:156
  247.4 72.3 %copy-start.32 = (s32[256]{0:T(256)S(1)}, s32[256]{0:T(256)}, u32[]{:S(2)}) copy-start(s32[256]{0:T(256)} %copy-done.31) | copy-start | bytes 3076
  247.4 72.5 %copy-start.33 = (s32[1,128,2]{1,2,0:T(2,128)S(1)}, s32[1,128,2]{1,2,0:T(2,128)}, u32[]{:S(2)}) copy-start(s32[1,128,2]{1,2,0:T(2,128)} %param.12) | copy-start | bytes 3076
  309.9 58.0 %all-to-all-start.1 = ((bf16[32,16,2048]{2,1,0:T(8,128)(2,1)}), bf16[32,16,2048]{2,1,0:T(8,128)(2,1)S(1)}, u32[]{:S(2)}, u32[]{:S(2)}) async-start(bf16[32,16,2048]{2,1,0:T(8,128)(2,1)} %bitcast.187), calls=%async_computation.3 | async-start | bytes 4194304 | tf_op jit(solution)/shard_map/all_to_all | solution.py:158
  319.5 94.4 %all-gather.16.cloned.1.call-start = ((), (), s32[]{:S(2)}) async-start(), calls=%async_computation.8 | async-start | bytes 1310720 | tf_op jit(solution)/shard_map/all_gather | solution.py:183
  391.5 84.6 %all-gather.18.cloned.1.call-start = ((), (), s32[]{:S(2)}) async-start(), calls=%async_computation.9 | async-start | bytes 2359296 | tf_op jit(solution)/shard_map/all_gather | solution.py:183
  422.9 23.8 %collective-permute-start.5 = (bf16[512,1024]{1,0:T(8,128)(2,1)}, bf16[512,1024]{1,0:T(8,128)(2,1)}, u32[]{:S(2)}, u32[]{:S(2)}) collective-permute-start(bf16[512,1024]{1,0:T(8,128)(2,1)} %fusion.11), channel_id=1, source_target_pairs={{0,1},{1,0},{2,3},{3,2},{4,5},{5,4},{6,7},{7,6},{8,9},{9,8},{10,11... | collective-permute-start | bytes 3145736 | tf_op jit(solution)/shard_map/ppermute | solution.py:146
  430.1 39.0 %collective-permute-start.4 = (bf16[1024,512]{1,0:T(8,128)(2,1)S(1)}, bf16[1024,512]{1,0:T(8,128)(2,1)}, u32[]{:S(2)}, u32[]{:S(2)}) collective-permute-start(bf16[1024,512]{1,0:T(8,128)(2,1)S(1)} %fusion.8), channel_id=1, source_target_pairs={{0,1},{1,0},{2,3},{3,2},{4,5},{5,4},{6,7},{7,6},{8,9},{9,8},{10,11... | collective-permute-start | bytes 3145736 | tf_op jit(solution)/shard_map/ppermute | solution.py:145
  430.5 42.7 %copy-start.10 = (f32[1,1024]{1,0:T(1,128)S(1)}, f32[1,1024]{1,0:T(1,128)}, u32[]{:S(2)}) copy-start(f32[1,1024]{1,0:T(1,128)} %copy-done.9) | copy-start | bytes 12292
  430.5 42.7 %copy-start.12 = (f32[1,1024]{1,0:T(1,128)S(1)}, f32[1,1024]{1,0:T(1,128)}, u32[]{:S(2)}) copy-start(f32[1,1024]{1,0:T(1,128)} %copy-done.11) | copy-start | bytes 12292
  430.5 42.7 %copy-start.14 = (f32[1,1024]{1,0:T(1,128)S(1)}, f32[1,1024]{1,0:T(1,128)}, u32[]{:S(2)}) copy-start(f32[1,1024]{1,0:T(1,128)} %copy-done.13) | copy-start | bytes 12292
  430.5 42.7 %copy-start.16 = (f32[1,1024]{1,0:T(1,128)S(1)}, f32[1,1024]{1,0:T(1,128)}, u32[]{:S(2)}) copy-start(f32[1,1024]{1,0:T(1,128)} %copy-done.15) | copy-start | bytes 12292
  430.5 42.7 %copy-start.18 = (f32[1,1024]{1,0:T(1,128)S(1)}, f32[1,1024]{1,0:T(1,128)}, u32[]{:S(2)}) copy-start(f32[1,1024]{1,0:T(1,128)} %copy-done.17) | copy-start | bytes 12292
  430.5 42.7 %copy-start.20 = (f32[1,1024]{1,0:T(1,128)S(1)}, f32[1,1024]{1,0:T(1,128)}, u32[]{:S(2)}) copy-start(f32[1,1024]{1,0:T(1,128)} %copy-done.19) | copy-start | bytes 12292
  430.5 42.7 %copy-start.22 = (f32[1,1024]{1,0:T(1,128)S(1)}, f32[1,1024]{1,0:T(1,128)}, u32[]{:S(2)}) copy-start(f32[1,1024]{1,0:T(1,128)} %copy-done.21) | copy-start | bytes 12292
  430.5 42.7 %copy-start.24 = (f32[1,1024]{1,0:T(1,128)S(1)}, f32[1,1024]{1,0:T(1,128)}, u32[]{:S(2)}) copy-start(f32[1,1024]{1,0:T(1,128)} %copy-done.23) | copy-start | bytes 12292
  430.5 42.7 %copy-start.26 = (f32[1,1024]{1,0:T(1,128)S(1)}, f32[1,1024]{1,0:T(1,128)}, u32[]{:S(2)}) copy-start(f32[1,1024]{1,0:T(1,128)} %copy-done.25) | copy-start | bytes 12292
  430.6 42.7 %copy-start.28 = (f32[1,1024]{1,0:T(1,128)S(1)}, f32[1,1024]{1,0:T(1,128)}, u32[]{:S(2)}) copy-start(f32[1,1024]{1,0:T(1,128)} %copy-done.27) | copy-start | bytes 12292
  430.6 42.7 %copy-start.30 = (f32[1,1024]{1,0:T(1,128)S(1)}, f32[1,1024]{1,0:T(1,128)}, u32[]{:S(2)}) copy-start(f32[1,1024]{1,0:T(1,128)} %copy-done.29) | copy-start | bytes 12292
  450.0 22.1 %collective-permute-start.2 = (bf16[15,1024]{1,0:T(8,128)(2,1)S(1)}, bf16[15,1024]{1,0:T(8,128)(2,1)S(1)}, u32[]{:S(2)}, u32[]{:S(2)}) collective-permute-start(bf16[15,1024]{1,0:T(8,128)(2,1)S(1)} %get-tuple-element.49), channel_id=1, source_target_pairs={{0,2},{2,4},{4,6},{6,8},{8,10},{10,12},{12,14},{14,16},{16,18},{18... | collective-permute-start | bytes 92168 | tf_op jit(solution)/shard_map/ppermute | solution.py:18
  459.8 13.3 %collective-permute-start.3 = (bf16[15,1024]{1,0:T(8,128)(2,1)S(1)}, bf16[15,1024]{1,0:T(8,128)(2,1)S(1)}, u32[]{:S(2)}, u32[]{:S(2)}) collective-permute-start(bf16[15,1024]{1,0:T(8,128)(2,1)S(1)} %get-tuple-element.50), channel_id=1, source_target_pairs={{2,0},{4,2},{6,4},{8,6},{10,8},{12,10},{14,12},{16,14},{18,16},{20... | collective-permute-start | bytes 92168 | tf_op jit(solution)/shard_map/ppermute | solution.py:19
  473.3 13.9 %copy-start.1 = (bf16[1,512,1024]{2,1,0:T(8,128)(2,1)S(1)}, bf16[1,512,1024]{2,1,0:T(8,128)(2,1)}, u32[]{:S(2)}) copy-start(bf16[1,512,1024]{2,1,0:T(8,128)(2,1)} %param.14) | copy-start | bytes 3145732
  (32 other events, 230.9 us)
Sparse Core Ops, SparseCore 0:
  94.1 63.4 all-gather.11
  159.4 27.0 all-gather.13
  224.5 22.9 reduce-scatter.2
  249.8 60.0 reduce-scatter.4
  391.6 22.2 all-gather.15
  416.0 39.1 all-gather.17
